TPU v7x, 256 devices: a whole 4x4x8 slice. The times are simulated.
256 devices in a mesh: row: 32 (over z, x_lo, core), feat: 8 (over y, x_hi).
Axes of the slice: x: 4 (x_hi: 2, x_lo: 2; x = x_hi * 2 + x_lo), y: 4, z: 8, core: 2. Of those that a mesh axis runs over, the one named last changes fastest.
Arguments:
- vectors: bfloat16 [81920, 1024], P('row', 'feat')
- rotation: bfloat16 [1024, 1024], P('feat')
- codes: int32 [81920, 64], P('row', 'feat'), may hold values from 0 to 255
- live_rows: int32 [32], P('row'), may hold values from 640 to 2560
Outputs:
- centroids: float32 [256, 1024], P('row', 'feat')
- grad_t: float32 [1024, 1024], P('row', 'feat')
All inputs are finite; a program needn't handle non-finite values.
Results may differ from a plain program's by a relative error of at most 0.00094.
Values may be sent and summed in bfloat16 or wider, within the bound.
No kernel may reach another device: no remote copies, remote signals or barrier semaphores. Data moves between devices by JAX's collectives and lax.ppermute only.
A program may use at most 64 MiB of HBM per device.

v0:
```python
import math
import jax
import jax.numpy as jnp
from jax import lax
from jax.sharding import PartitionSpec as P

K = 256


def make_hot(code_block, keeper):
    kinds = jnp.arange(K, dtype=jnp.int32)
    return (code_block[:, :, None] == kinds[None, None, :]).astype(jnp.bfloat16) * keeper[
        :, None, None
    ]


def rebuild(hot, table_part, groups, depth):
    rows = hot.shape[0]
    shaped = table_part.reshape(K, groups, depth)
    joined = jnp.einsum("nmk,kmd->nmd", hot, shaped, preferred_element_type=jnp.float32)
    return joined.reshape(rows, groups * depth).astype(jnp.bfloat16)


def blocked_sums(hot, rotated, groups, depth):
    rows = hot.shape[0]
    step_rows = math.gcd(rows, 512)
    turns = rows // step_rows

    def add_block(index, total):
        hot_block = lax.dynamic_slice_in_dim(hot, index * step_rows, step_rows, 0).astype(
            jnp.float32
        )
        rot_block = lax.dynamic_slice_in_dim(rotated, index * step_rows, step_rows, 0).reshape(
            step_rows, groups, depth
        )
        return total + jnp.einsum(
            "nmk,nmd->kmd", hot_block, rot_block, precision=lax.Precision.HIGHEST
        )

    start = jnp.zeros((K, groups, depth), jnp.float32)
    return lax.fori_loop(0, turns, add_block, start).reshape(K, groups * depth)


def shards(vectors, rotation, codes, live_rows):
    rows = vectors.shape[0]
    local = vectors.shape[1]
    groups = codes.shape[1]
    depth = local // groups
    keeper = (jnp.arange(rows, dtype=jnp.int32) < live_rows[0]).astype(jnp.bfloat16)
    hot = make_hot(codes, keeper)
    counts = jnp.sum(hot, axis=0, dtype=jnp.float32).T
    partial_value = jnp.dot(vectors, rotation, preferred_element_type=jnp.float32)
    rotated = lax.psum_scatter(partial_value, "feat", scatter_dimension=1, tiled=True)
    sums = blocked_sums(hot, rotated, groups, depth)
    share_sums, share_counts = (
        lax.psum_scatter(sums, "row", scatter_dimension=0, tiled=True),
        lax.psum_scatter(counts, "row", scatter_dimension=0, tiled=True),
    )
    centroids = share_sums / (jnp.repeat(share_counts, depth, axis=1) + 1.0)
    table = lax.all_gather(centroids.astype(jnp.bfloat16), "row", axis=0, tiled=True)
    local_recon = rebuild(hot, table, groups, depth)
    recon = lax.all_gather(local_recon, "feat", axis=1, tiled=True)
    inverse = 1.0 / (rows * lax.axis_size("row"))
    product = lax.dot_general(
        recon, vectors, (((0,), (0,)), ((), ())), preferred_element_type=jnp.float32
    )
    grad_t = lax.psum_scatter(product * inverse, "row", scatter_dimension=0, tiled=True)
    return (centroids, grad_t)


def solution(mesh):
    return jax.shard_map(
        shards,
        mesh=mesh,
        in_specs=(P("row", "feat"), P("feat", None), P("row", "feat"), P("row")),
        out_specs=(P("row", "feat"), P("row", "feat")),
        check_vma=False,
    )
```

profile of v0, /device:TPU:4, one launch (start us, length us, event | category | flops | bytes accessed | tf_op | source)
XLA Modules:
  0.0 625.4 jit_solution(6406891080240727840)
XLA Ops:
  7.2 0.0 copy-start
  7.2 0.0 copy-start.2
  7.2 0.0 reduce-scatter.5.cloned.1.call-start
  7.2 1.0 copy-done
  8.3 6.4 %fusion.20 = f32[2560,1024]{1,0:T(8,128)} fusion(bf16[2560,128]{1,0:T(8,128)(2,1)S(1)} %copy-done, bf16[128,1024]{1,0:T(8,128)(2,1)} %param.7), kind=kOutput, calls=%fused_computation.20 | convolution fusion | flops 671088640 | bytes 11403264 | tf_op jit(solution)/shard_map/dot_general | solution.py:52
  14.7 0.0 reduce-scatter.5.cloned.1.call-update
  14.7 0.0 all-reduce.4.cloned.1.call-start
  15.4 0.0 copy-done.2
  15.4 5.4 fusion.9
  20.9 0.0 copy-start.3
  20.9 133.1 %reduce-scatter.5.cloned.1.call-done = f32[2560,128]{1,0:T(8,128)} async-done(((f32[2560,1024]{1,0:T(8,128)}), f32[2560,128]{1,0:T(8,128)}) %reduce-scatter.5.cloned.1.call-update) | async-done | bytes 1310736 | tf_op jit(solution)/shard_map/reduce_scatter | solution.py:53
  153.9 18.3 %while.14 = (s32[]{:T(128)}, f32[256,8,16]{0,2,1:T(8,128)S(1)}, f32[2560,128]{1,0:T(8,128)}, bf16[2560,8,256]{2,0,1:T(8,128)(2,1)}, s32[]{:T(128)}, /*index=5*/s32[]{:T(128)}, s32[]{:T(128)}, s32[]{:T(128)}) while((s32[]{:T(128)}, f32[256,8,16]{0,2,1:T(8,128)S(1)}, f32[2560,128]{1,0:T(8,128)}, bf16[2560,8,256]{2,0,1:T(8,128)(2,1)}, ...), condition=%wide.region_2.0_spmd.clone, body=%wide.region_1.0_spmd.clone.sunk | while | flops 201392128 | bytes 3670173 | solution.py:41
  153.9 1.0 constant_dynamic-slice_fusion.2
  154.9 0.1 copy.21
  155.1 2.5 fusion.32
  157.6 1.0 constant_dynamic-slice_fusion.2
  158.6 0.1 copy.21
  158.7 2.5 fusion.32
  161.3 1.0 constant_dynamic-slice_fusion.2
  162.3 0.1 copy.21
  162.4 2.5 fusion.32
  164.9 1.0 constant_dynamic-slice_fusion.2
  165.9 0.1 copy.21
  166.1 2.5 fusion.32
  168.6 1.0 constant_dynamic-slice_fusion.2
  169.6 0.1 copy.21
  169.7 2.5 fusion.32
  172.3 0.6 copy-done.1
  172.9 0.0 all-reduce.4.cloned.1.call-update
  172.9 0.0 all-gather.2.cloned.1.call-start
  173.0 4.6 convert_reduce_fusion
  177.6 0.0 copy-done.3
  177.6 0.6 dynamic-slice
  178.9 57.8 %all-reduce.1 = f32[256,8]{0,1:T(8,128)S(1)} all-reduce(f32[256,8]{0,1:T(8,128)S(1)} %bitcast.37), channel_id=4, replica_groups=mesh['row'=32,'feat'=8] {'row'}, use_global_device_ids=true, to_apply=%region_5.0.clone | all-reduce | flops 2048 | bytes 16384
  236.7 0.1 dynamic-slice_add_fusion
  236.8 138.9 %all-reduce.4.cloned.1.call-done = f32[256,128]{0,1:T(8,128)} async-done(((f32[256,128]{0,1:T(8,128)}), f32[256,128]{0,1:T(8,128)}) %all-reduce.4.cloned.1.call-update) | async-done | bytes 131088
  375.6 0.9 fusion.19
  376.5 0.1 copy.12
  376.6 30.6 %all_gather.6 = bf16[256,128]{1,0:T(8,128)(2,1)S(1)} all-gather(bf16[8,128]{1,0:T(8,128)(2,1)S(1)} %copy.12), channel_id=1, replica_groups=mesh['row'=32,'feat'=8] {'row'}, dimensions={0}, use_global_device_ids=true | all-gather | bytes 67584 | tf_op jit(solution)/shard_map/all_gather | solution.py:60
  407.2 0.1 copy.13
  407.3 6.3 %fusion.14 = bf16[8,16,2560]{2,1,0:T(8,128)(2,1)} fusion(bf16[256,8,16]{0,2,1:T(8,128)(2,1)S(1)} %bitcast.36, s32[2560,8]{0,1:T(8,128)S(1)} %copy-done.2, bf16[2560]{0:T(1024)(128)(2,1)S(1)} %fusion.17), kind=kOutput, calls=%fused_computation.12 | convolution fusion | flops 178585600 | bytes 807936 | tf_op jit(solution)/shard_map/nmk,kmd->nmd/dot_general | solution.py:20
  413.6 0.0 all-gather.2.cloned.1.call-update
  413.6 0.0 reduce-scatter.7.cloned.1.call-start
  413.7 84.3 %all-gather.2.cloned.1.call-done = bf16[2560,1024]{0,1:T(8,128)(2,1)} async-done(((bf16[2560,128]{0,1:T(8,128)(2,1)}), bf16[2560,1024]{0,1:T(8,128)(2,1)}) %all-gather.2.cloned.1.call-update) | async-done | bytes 5242896 | tf_op jit(solution)/shard_map/all_gather | solution.py:62
  497.9 4.8 convolution_multiply_fusion
  502.8 0.0 reduce-scatter.7.cloned.1.call-update
  502.8 0.7 copy.14
  503.4 115.5 %reduce-scatter.7.cloned.1.call-done = f32[32,128]{1,0:T(8,128)} async-done(((f32[1024,128]{1,0:T(8,128)}), f32[32,128]{1,0:T(8,128)}) %reduce-scatter.7.cloned.1.call-update) | async-done | bytes 16400 | tf_op jit(solution)/shard_map/reduce_scatter | solution.py:67
  (3 shorter events, 0.0 us)
Async XLA Ops:
  7.2 1.1 copy-start
  7.2 8.3 %copy-start.2 = (s32[2560,8]{0,1:T(8,128)S(1)}, s32[2560,8]{0,1:T(8,128)}, u32[]{:S(2)}) copy-start(s32[2560,8]{0,1:T(8,128)} %param.8) | copy-start | bytes 245764
  7.2 146.8 %reduce-scatter.5.cloned.1.call-start = ((), (), s32[]{:S(2)}) async-start(), calls=%async_computation.2 | async-start | bytes 11796480 | tf_op jit(solution)/shard_map/reduce_scatter | solution.py:53
  14.7 360.9 %all-reduce.4.cloned.1.call-start = ((), (), s32[]{:S(2)}) async-start(), calls=%async_computation.5 | async-start | bytes 262144
  20.9 156.7 %copy-start.3 = (u32[256]{0:T(256)S(1)}, u32[256]{0:T(256)}, u32[]{:S(2)}) copy-start(u32[256]{0:T(256)} %constant.42) | copy-start | bytes 3076
  172.3 0.6 copy-start.1
  172.9 325.0 %all-gather.2.cloned.1.call-start = ((), (), s32[]{:S(2)}) async-start(), calls=%async_computation.3 | async-start | bytes 5898240 | tf_op jit(solution)/shard_map/all_gather | solution.py:62
  413.6 205.3 %reduce-scatter.7.cloned.1.call-start = ((), (), s32[]{:S(2)}) async-start(), calls=%async_computation.4 | async-start | bytes 540672 | tf_op jit(solution)/shard_map/reduce_scatter | solution.py:67
Sparse Core Ops, SparseCore 0:
  14.8 139.0 reduce-scatter.4
  173.1 202.5 all-reduce.3
  413.7 84.1 all-gather.1
  502.9 115.9 reduce-scatter.6
where the time goes:
time: 626 us; the launch traced here: 625 us
  waiting for transfers between devices  472 us (75%)
  blocking collectives  88.4 us (14%)
  matrix products  30.3 us (5%)
  between operations  15.1 us (2%)
  other arithmetic  11.1 us (2%)
  local copies, waits for them, and re-layouts  8.63 us (1%)
    unnamed x5, waiting for transfers between devices  139 us
    reduce_scatter x1, waiting for transfers between devices, shards(): lax.psum_scatter(partial_value, 'feat', scatter_dimension=1, tiled=True)  133 us
    reduce_scatter x1, waiting for transfers between devices, shards(): lax.psum_scatter(product * inverse, 'row', scatter_dimension=0, tiled=True)  115 us
    all_gather x1, waiting for transfers between devices, shards(): recon = lax.all_gather(local_recon, 'feat', axis=1, tiled=True)  84.3 us
    unnamed x1, blocking collectives  57.8 us
    all_gather x1, blocking collectives, shards(): lax.all_gather(centroids.astype(jnp.bfloat16), 'row', axis=0, tiled=True)  30.6 us
    dot_general x5, matrix products, add_block(): jnp.einsum('nmk,nmd->kmd', hot_block, rot_block, precision=lax.Precision....  12.7 us
  transfers between devices with their start and end apart: 4, of which 4 were waited for; matrix products, arithmetic and copies ran while one was open for 2% of the time, Pallas kernels for 0%

commit v1 on v0

--- a/solution.py
+++ b/solution.py
@@ -59,7 +59,9 @@
     centroids = share_sums / (jnp.repeat(share_counts, depth, axis=1) + 1.0)
     table = lax.all_gather(centroids.astype(jnp.bfloat16), "row", axis=0, tiled=True)
     local_recon = rebuild(hot, table, groups, depth)
-    recon = lax.all_gather(local_recon, "feat", axis=1, tiled=True)
+    recon = jnp.concatenate(
+        lax.all_to_all(jnp.stack([local_recon] * lax.axis_size("feat")), "feat", 0, 0), axis=1
+    )
     inverse = 1.0 / (rows * lax.axis_size("row"))
     product = lax.dot_general(
         recon, vectors, (((0,), (0,)), ((), ())), preferred_element_type=jnp.float32

time: 626 us -> 607 us (0.970)
  waiting for transfers between devices: 472 us -> 386 us
  blocking collectives: 88.4 us -> 155 us
    all_gather x1 -> x0, waiting for transfers between devices: 84.3 us -> none  [shards(): recon = lax.all_gather(local_recon, 'feat', axis=1, tiled=True)]
    all_to_all x0 -> x1, blocking collectives: none -> 67 us  [shards(): lax.all_to_all(jnp.stack([local_recon] * lax.axis_size('feat')), 'feat',...]
    unnamed x5 -> x4, waiting for transfers between devices: 139 us -> 139 us
  transfers between devices with their start and end apart: 4 -> 3, of which waited for: 4 -> 3; matrix products, arithmetic and copies ran while one was open for 2% -> 2% of each run, Pallas kernels for 0% -> 0%
where the time goes in v1:
time: 607 us; the launch traced here: 606 us
  waiting for transfers between devices  386 us (64%)
  blocking collectives  155 us (26%)
  matrix products  28.6 us (5%)
  between operations  15.1 us (2%)
  other arithmetic  11.1 us (2%)
  local copies, waits for them, and re-layouts  9.08 us (1%)
    unnamed x4, waiting for transfers between devices  139 us
    reduce_scatter x1, waiting for transfers between devices, shards(): lax.psum_scatter(partial_value, 'feat', scatter_dimension=1, tiled=True)  133 us
    reduce_scatter x1, waiting for transfers between devices, shards(): lax.psum_scatter(product * inverse, 'row', scatter_dimension=0, tiled=True)  114 us
    all_to_all x1, blocking collectives, shards(): lax.all_to_all(jnp.stack([local_recon] * lax.axis_size('feat')), 'feat',...  67 us
    unnamed x1, blocking collectives  57.8 us
    all_gather x1, blocking collectives, shards(): lax.all_gather(centroids.astype(jnp.bfloat16), 'row', axis=0, tiled=True)  30.6 us
    dot_general x5, matrix products, add_block(): jnp.einsum('nmk,nmd->kmd', hot_block, rot_block, precision=lax.Precision....  12.7 us
  transfers between devices with their start and end apart: 3, of which 3 were waited for; matrix products, arithmetic and copies ran while one was open for 2% of the time, Pallas kernels for 0%

profile of v1, /device:TPU:4, one launch (start us, length us, event | category | flops | bytes accessed | tf_op | source)
XLA Modules:
  0.0 605.7 jit_solution(12096597548809295441)
XLA Ops:
  7.2 0.0 copy-start
  7.2 0.0 copy-start.2
  7.2 0.0 reduce-scatter.5.cloned.1.call-start
  7.2 1.0 copy-done
  8.3 6.4 %fusion.20 = f32[2560,1024]{1,0:T(8,128)} fusion(bf16[2560,128]{1,0:T(8,128)(2,1)S(1)} %copy-done, bf16[128,1024]{1,0:T(8,128)(2,1)} %param.7), kind=kOutput, calls=%fused_computation.20 | convolution fusion | flops 671088640 | bytes 11403264 | tf_op jit(solution)/shard_map/dot_general | solution.py:52
  14.7 0.0 reduce-scatter.5.cloned.1.call-update
  14.7 0.0 all-reduce.4.cloned.1.call-start
  15.4 0.0 copy-done.2
  15.5 5.5 fusion.9
  20.9 0.0 copy-start.3
  20.9 133.0 %reduce-scatter.5.cloned.1.call-done = f32[2560,128]{1,0:T(8,128)} async-done(((f32[2560,1024]{1,0:T(8,128)}), f32[2560,128]{1,0:T(8,128)}) %reduce-scatter.5.cloned.1.call-update) | async-done | bytes 1310736 | tf_op jit(solution)/shard_map/reduce_scatter | solution.py:53
  154.0 18.3 %while.14 = (s32[]{:T(128)}, f32[256,8,16]{0,2,1:T(8,128)S(1)}, f32[2560,128]{1,0:T(8,128)}, bf16[2560,8,256]{2,0,1:T(8,128)(2,1)}, s32[]{:T(128)}, /*index=5*/s32[]{:T(128)}, s32[]{:T(128)}, s32[]{:T(128)}) while((s32[]{:T(128)}, f32[256,8,16]{0,2,1:T(8,128)S(1)}, f32[2560,128]{1,0:T(8,128)}, bf16[2560,8,256]{2,0,1:T(8,128)(2,1)}, ...), condition=%wide.region_2.0_spmd.clone, body=%wide.region_1.0_spmd.clone.sunk | while | flops 201392128 | bytes 3670173 | solution.py:41
  154.0 1.0 constant_dynamic-slice_fusion.2
  154.9 0.1 copy.22
  155.1 2.5 fusion.32
  157.6 1.0 constant_dynamic-slice_fusion.2
  158.6 0.1 copy.22
  158.7 2.5 fusion.32
  161.3 1.0 constant_dynamic-slice_fusion.2
  162.3 0.1 copy.22
  162.4 2.5 fusion.32
  165.0 1.0 constant_dynamic-slice_fusion.2
  165.9 0.1 copy.22
  166.1 2.5 fusion.32
  168.6 1.0 constant_dynamic-slice_fusion.2
  169.6 0.1 copy.22
  169.7 2.5 fusion.32
  172.3 0.0 copy-start.1
  172.3 0.7 copy-done.1
  173.0 0.0 all-reduce.4.cloned.1.call-update
  173.0 0.0 reduce-scatter.7.cloned.1.call-start
  173.0 4.6 convert_reduce_fusion
  177.7 0.0 copy-done.3
  177.7 0.6 dynamic-slice
  178.9 57.8 %all-reduce.1 = f32[256,8]{0,1:T(8,128)S(1)} all-reduce(f32[256,8]{0,1:T(8,128)S(1)} %bitcast.41), channel_id=4, replica_groups=mesh['row'=32,'feat'=8] {'row'}, use_global_device_ids=true, to_apply=%region_5.0.clone | all-reduce | flops 2048 | bytes 16384
  236.7 0.1 dynamic-slice_add_fusion
  236.8 138.9 %all-reduce.4.cloned.1.call-done = f32[256,128]{0,1:T(8,128)} async-done(((f32[256,128]{0,1:T(8,128)}), f32[256,128]{0,1:T(8,128)}) %all-reduce.4.cloned.1.call-update) | async-done | bytes 131088
  375.6 0.9 fusion.19
  376.6 0.1 copy.13
  376.6 30.6 %all_gather.3 = bf16[256,128]{1,0:T(8,128)(2,1)S(1)} all-gather(bf16[8,128]{1,0:T(8,128)(2,1)S(1)} %copy.13), channel_id=1, replica_groups=mesh['row'=32,'feat'=8] {'row'}, dimensions={0}, use_global_device_ids=true | all-gather | bytes 67584 | tf_op jit(solution)/shard_map/all_gather | solution.py:60
  407.2 0.1 copy.14
  407.3 7.1 %fusion.14 = bf16[8,16,2560]{2,1,0:T(8,128)(2,1)S(1)} fusion(bf16[256,8,16]{0,2,1:T(8,128)(2,1)S(1)} %bitcast.40, s32[2560,8]{0,1:T(8,128)S(1)} %copy-done.2, bf16[2560]{0:T(1024)(128)(2,1)S(1)} %fusion.17), kind=kOutput, calls=%fused_computation.12 | convolution fusion | flops 178585600 | bytes 807936 | tf_op jit(solution)/shard_map/nmk,kmd->nmd/dot_general | solution.py:20
  414.5 0.4 stack.2
  414.9 67.0 %all_to_all.5 = bf16[8,2560,128]{1,2,0:T(8,128)(2,1)S(1)} all-to-all(bf16[8,2560,128]{1,2,0:T(8,128)(2,1)S(1)} %stack.2), channel_id=1, replica_groups=mesh['row'=32,'feat'=8] {'feat'}, dimensions={0} | all-to-all | bytes 10485760 | tf_op jit(solution)/shard_map/all_to_all | solution.py:63
  481.9 2.3 convolution_multiply_fusion
  484.2 0.0 reduce-scatter.7.cloned.1.call-update
  484.3 0.7 copy.15
  484.9 114.2 %reduce-scatter.7.cloned.1.call-done = f32[32,128]{1,0:T(8,128)} async-done(((f32[1024,128]{1,0:T(8,128)}), f32[32,128]{1,0:T(8,128)}) %reduce-scatter.7.cloned.1.call-update) | async-done | bytes 16400 | tf_op jit(solution)/shard_map/reduce_scatter | solution.py:69
  (2 shorter events, 0.0 us)
Async XLA Ops:
  7.2 1.1 copy-start
  7.2 8.3 %copy-start.2 = (s32[2560,8]{0,1:T(8,128)S(1)}, s32[2560,8]{0,1:T(8,128)}, u32[]{:S(2)}) copy-start(s32[2560,8]{0,1:T(8,128)} %param.8) | copy-start | bytes 245764
  7.2 146.8 %reduce-scatter.5.cloned.1.call-start = ((), (), s32[]{:S(2)}) async-start(), calls=%async_computation.3 | async-start | bytes 11796480 | tf_op jit(solution)/shard_map/reduce_scatter | solution.py:53
  14.7 360.9 %all-reduce.4.cloned.1.call-start = ((), (), s32[]{:S(2)}) async-start(), calls=%async_computation.5 | async-start | bytes 262144
  20.9 156.7 %copy-start.3 = (u32[256]{0:T(256)S(1)}, u32[256]{0:T(256)}, u32[]{:S(2)}) copy-start(u32[256]{0:T(256)} %constant.42) | copy-start | bytes 3076
  172.3 0.7 copy-start.1
  173.0 426.2 %reduce-scatter.7.cloned.1.call-start = ((), (), s32[]{:S(2)}) async-start(), calls=%async_computation.4 | async-start | bytes 540672 | tf_op jit(solution)/shard_map/reduce_scatter | solution.py:69
Sparse Core Ops, SparseCore 0:
  14.8 139.0 reduce-scatter.4
  173.1 202.5 all-reduce.3
  484.4 114.6 reduce-scatter.6
